TPU v7x, 512 devices: a whole 4x8x8 slice. The times are simulated.
512 devices in a mesh: ctx: 128 (over z_hi, x, y), head: 4 (over z_lo, core).
Axes of the slice: x: 4, y: 8, z: 8 (z_hi: 4, z_lo: 2; z = z_hi * 2 + z_lo), core: 2. Of those that a mesh axis runs over, the one named last changes fastest.
Arguments:
- queries: bfloat16 [32768, 4096], P(('ctx', 'head')), may hold values from -200 to 200
- normed_key_state: bfloat16 [32768, 2048], P(('ctx', 'head')), may hold values from -5 to 5
- value_state_rows: bfloat16 [32768, 2048], P(('ctx', 'head')), may hold values from -6 to 6
- output_gradient: bfloat16 [32768, 4096], P(('ctx', 'head')), may hold values from -6 to 6
- doc_start: int32 [32768], P('ctx'), may hold values from 0 to 32767, as said below
Outputs:
- grad_queries: bfloat16 [32768, 4096], P(('ctx', 'head'))
- key_gradient: bfloat16 [32768, 2048], P(('ctx', 'head'))
- value_gradient: bfloat16 [32768, 2048], P(('ctx', 'head'))
Inputs may be any that keep to these rules, and one draw needn't show every extreme that they name: doc_start[t] is the first position of the document that holds token t: doc_start[0] = 0, each doc_start[t] equals t or doc_start[t - 1], and the last token, position 32767, begins a document of its own.
All inputs are finite; a program needn't handle non-finite values.
Results may differ from a plain program's by a relative error of at most 0.007.
Values may be sent and summed in bfloat16 or wider, within the bound.
No kernel may reach another device: no remote copies, remote signals or barrier semaphores. Data moves between devices by JAX's collectives and lax.ppermute only.
A program may use at most 64 MiB of HBM per device.

v0:
```python
import jax
import jax.numpy as jnp
from jax import lax
from jax.sharding import PartitionSpec as P

QUERY_HEADS = 32
KEY_VALUE_HEADS = 16
HEAD_SIZE = 128
WINDOW = 512
SPAN = 2
score_scale = 168.0 ** (-0.5)


def passed_along(block, axis, distance):
    devices = range(lax.axis_size(axis))
    route = [(i - distance, i) for i in devices if i - distance in devices]
    return lax.ppermute(block, axis, route)


def pair_scores(query_heads, key_block):
    return score_scale * jnp.einsum(
        "tgjd,kgd->gjtk", query_heads, key_block, preferred_element_type=jnp.float32
    )


def local(queries, normed_key_state, value_state_rows, output_gradient, doc_start):
    query_loc, key_loc, value_loc, grad_loc = (
        lax.all_to_all(queries, "head", split_axis=1, concat_axis=0, tiled=True),
        lax.all_to_all(normed_key_state, "head", split_axis=1, concat_axis=0, tiled=True),
        lax.all_to_all(value_state_rows, "head", split_axis=1, concat_axis=0, tiled=True),
        lax.all_to_all(output_gradient, "head", split_axis=1, concat_axis=0, tiled=True),
    )
    tok_rows = query_loc.shape[0]
    kv_groups = key_loc.shape[1] // HEAD_SIZE
    group_share = QUERY_HEADS // KEY_VALUE_HEADS
    query_heads = query_loc.reshape(tok_rows, kv_groups, group_share, HEAD_SIZE)
    grad_heads = grad_loc.reshape(tok_rows, kv_groups, group_share, HEAD_SIZE)
    kv_local = jnp.stack([key_loc, value_loc])
    kv_blocks = [kv_local]
    for distance in range(1, SPAN + 1):
        kv_blocks.append(passed_along(kv_local, "ctx", distance))
    shard_index = lax.axis_index("ctx")
    local_iota = jnp.arange(tok_rows, dtype=jnp.int32)
    query_pos = shard_index * tok_rows + local_iota

    def visible(distance):
        key_pos = (shard_index - distance) * tok_rows + local_iota
        return (
            (key_pos[None, :] >= doc_start[:, None])
            & (key_pos[None, :] <= query_pos[:, None])
            & (query_pos[:, None] - key_pos[None, :] < WINDOW)
        )

    def unpack(kv_block):
        return (
            kv_block[0].reshape(tok_rows, kv_groups, HEAD_SIZE),
            kv_block[1].reshape(tok_rows, kv_groups, HEAD_SIZE),
        )

    masks = [visible(distance) for distance in range(SPAN + 1)]
    stat_shape = (kv_groups, group_share, tok_rows)
    running = (
        jnp.full(stat_shape, -jnp.inf, jnp.float32),
        jnp.zeros(stat_shape, jnp.float32),
        jnp.zeros(stat_shape, jnp.float32),
    )
    for distance in range(SPAN + 1):
        gather_key_block, gather_value_block = unpack(kv_blocks[distance])
        gather_masked = jnp.where(
            masks[distance], pair_scores(query_heads, gather_key_block), -jnp.inf
        )
        gather_dprob = jnp.einsum(
            "tgjd,kgd->gjtk", grad_heads, gather_value_block, preferred_element_type=jnp.float32
        )
        new_max = jnp.maximum(running[0], jnp.max(gather_masked, axis=-1))
        factor = jnp.exp(running[0] - new_max)
        weights = jnp.exp(gather_masked - new_max[..., None])
        running = (
            new_max,
            running[1] * factor + jnp.sum(weights, axis=-1),
            running[2] * factor + jnp.sum(weights * gather_dprob, axis=-1),
        )
    log_total = running[0] + jnp.log(running[1])
    delta = running[2] / running[1]
    zero_parts = (
        jnp.zeros((tok_rows, kv_groups, group_share, HEAD_SIZE), jnp.float32),
        jnp.zeros((2, tok_rows, kv_groups * HEAD_SIZE), jnp.float32),
    )
    query_total = zero_parts[0]
    kv_parts = []
    for distance in range(SPAN + 1):
        key_block, value_block = unpack(kv_blocks[distance])
        masked = jnp.where(masks[distance], pair_scores(query_heads, key_block), -jnp.inf)
        prob = jnp.exp(masked - log_total[..., None])
        dprob = jnp.einsum(
            "tgjd,kgd->gjtk", grad_heads, value_block, preferred_element_type=jnp.float32
        )
        dscore = (prob * (dprob - delta[..., None])).astype(jnp.bfloat16)
        prob_half = prob.astype(jnp.bfloat16)
        query_part = score_scale * jnp.einsum(
            "gjtk,kgd->tgjd", dscore, key_block, preferred_element_type=jnp.float32
        )
        key_part = score_scale * jnp.einsum(
            "gjtk,tgjd->kgd", dscore, query_heads, preferred_element_type=jnp.float32
        )
        value_part = jnp.einsum(
            "gjtk,tgjd->kgd", prob_half, grad_heads, preferred_element_type=jnp.float32
        )
        query_part, kv_part = (
            query_part,
            jnp.stack([key_part, value_part]).reshape(2, tok_rows, kv_groups * HEAD_SIZE),
        )
        query_total = query_total + query_part
        kv_parts.append(kv_part)
    kv_total = kv_parts[0]
    for distance in range(1, SPAN + 1):
        kv_total = kv_total + passed_along(kv_parts[distance], "ctx", -distance)
    grad_query_loc = query_total.reshape(tok_rows, kv_groups * group_share * HEAD_SIZE).astype(
        jnp.bfloat16
    )
    grad_key_loc = kv_total[0].astype(jnp.bfloat16)
    grad_value_loc = kv_total[1].astype(jnp.bfloat16)
    return (
        lax.all_to_all(grad_query_loc, "head", split_axis=0, concat_axis=1, tiled=True),
        lax.all_to_all(grad_key_loc, "head", split_axis=0, concat_axis=1, tiled=True),
        lax.all_to_all(grad_value_loc, "head", split_axis=0, concat_axis=1, tiled=True),
    )


def solution(mesh):
    placed = (
        P(("ctx", "head"), None),
        P(("ctx", "head"), None),
        P(("ctx", "head"), None),
        P(("ctx", "head"), None),
        P("ctx"),
    )
    return jax.shard_map(
        local,
        mesh=mesh,
        in_specs=placed,
        out_specs=(P(("ctx", "head"), None), P(("ctx", "head"), None), P(("ctx", "head"), None)),
        check_vma=False,
    )
```

profile of v0, /device:TPU:54, one launch (start us, length us, event | category | flops | bytes accessed | tf_op | source)
XLA Modules:
  0.0 253.9 jit_solution(12213496482902532726)
XLA Ops:
  2.4 3.6 %all-to-all-start = ((bf16[64,4,512]{2,0,1:T(8,128)(2,1)}), bf16[64,4,512]{2,0,1:T(8,128)(2,1)S(1)}, u32[]{:S(2)}, u32[]{:S(2)}) async-start(bf16[64,4,512]{2,0,1:T(8,128)(2,1)} %bitcast.174), calls=%async_computation | async-start | bytes 524288 | tf_op jit(solution)/shard_map/all_to_all | solution.py:29
  7.7 4.3 %all-to-all-done = bf16[64,4,512]{2,0,1:T(8,128)(2,1)S(1)} async-done(((bf16[64,4,512]{2,0,1:T(8,128)(2,1)}), bf16[64,4,512]{2,0,1:T(8,128)(2,1)S(1)}, u32[]{:S(2)}, u32[]{:S(2)}) %all-to-all-start) | async-done | bytes 262176 | tf_op jit(solution)/shard_map/all_to_all | solution.py:29
  12.1 3.4 %all-to-all-start.2 = ((bf16[64,4,512]{2,0,1:T(8,128)(2,1)}), bf16[64,4,512]{2,0,1:T(8,128)(2,1)S(1)}, u32[]{:S(2)}, u32[]{:S(2)}) async-start(bf16[64,4,512]{2,0,1:T(8,128)(2,1)} %bitcast.173), calls=%async_computation.2 | async-start | bytes 524288 | tf_op jit(solution)/shard_map/all_to_all | solution.py:30
  16.3 5.1 %all-to-all-done.2 = bf16[64,4,512]{2,0,1:T(8,128)(2,1)S(1)} async-done(((bf16[64,4,512]{2,0,1:T(8,128)(2,1)}), bf16[64,4,512]{2,0,1:T(8,128)(2,1)S(1)}, u32[]{:S(2)}, u32[]{:S(2)}) %all-to-all-start.2) | async-done | bytes 262176 | tf_op jit(solution)/shard_map/all_to_all | solution.py:30
  21.4 3.5 %all-to-all-start.1 = ((bf16[64,4,1024]{2,0,1:T(8,128)(2,1)}), bf16[64,4,1024]{2,0,1:T(8,128)(2,1)S(1)}, u32[]{:S(2)}, u32[]{:S(2)}) async-start(bf16[64,4,1024]{2,0,1:T(8,128)(2,1)} %bitcast.172), calls=%async_computation.1 | async-start | bytes 1048576 | tf_op jit(solution)/shard_map/all_to_all | solution.py:28
  25.8 7.9 %all-to-all-done.1 = bf16[64,4,1024]{2,0,1:T(8,128)(2,1)S(1)} async-done(((bf16[64,4,1024]{2,0,1:T(8,128)(2,1)}), bf16[64,4,1024]{2,0,1:T(8,128)(2,1)S(1)}, u32[]{:S(2)}, u32[]{:S(2)}) %all-to-all-start.1) | async-done | bytes 524320 | tf_op jit(solution)/shard_map/all_to_all | solution.py:28
  33.7 3.5 %all-to-all-start.3 = ((bf16[64,4,1024]{2,0,1:T(8,128)(2,1)}), bf16[64,4,1024]{2,0,1:T(8,128)(2,1)S(1)}, u32[]{:S(2)}, u32[]{:S(2)}) async-start(bf16[64,4,1024]{2,0,1:T(8,128)(2,1)} %bitcast.171), calls=%async_computation.3 | async-start | bytes 1048576 | tf_op jit(solution)/shard_map/all_to_all | solution.py:31
  38.9 5.3 %collective-permute-start.1 = (bf16[2,256,512]{2,1,0:T(8,128)(2,1)}, bf16[2,256,512]{2,1,0:T(8,128)(2,1)}, u32[]{:S(2)}, u32[]{:S(2)}) collective-permute-start(bf16[2,256,512]{2,1,0:T(8,128)(2,1)} %pad_maximum_fusion.2), channel_id=1, source_target_pairs={{0,8},{4,12},{8,16},{12,20},{16,24},{20,28},{24,32},{28,36},{32,40... | collective-permute-start | bytes 1572872 | tf_op jit(solution)/shard_map/ppermute | solution.py:17
  44.3 3.5 %collective-permute-start = (bf16[2,256,512]{2,1,0:T(8,128)(2,1)}, bf16[2,256,512]{2,1,0:T(8,128)(2,1)}, u32[]{:S(2)}, u32[]{:S(2)}) collective-permute-start(bf16[2,256,512]{2,1,0:T(8,128)(2,1)} %pad_maximum_fusion.2), channel_id=1, source_target_pairs={{0,4},{4,8},{8,12},{12,16},{16,20},{20,24},{24,28},{28,32},{32,36}... | collective-permute-start | bytes 1572872 | tf_op jit(solution)/shard_map/ppermute | solution.py:17
  51.8 2.4 fusion.6
  54.2 14.3 %collective-permute-done.1 = bf16[2,256,512]{2,1,0:T(8,128)(2,1)} collective-permute-done((bf16[2,256,512]{2,1,0:T(8,128)(2,1)}, bf16[2,256,512]{2,1,0:T(8,128)(2,1)}, u32[]{:S(2)}, u32[]{:S(2)}) %collective-permute-start.1) | collective-permute-done | bytes 524320 | tf_op jit(solution)/shard_map/ppermute | solution.py:17
  74.0 5.3 %collective-permute-done = bf16[2,256,512]{2,1,0:T(8,128)(2,1)} collective-permute-done((bf16[2,256,512]{2,1,0:T(8,128)(2,1)}, bf16[2,256,512]{2,1,0:T(8,128)(2,1)}, u32[]{:S(2)}, u32[]{:S(2)}) %collective-permute-start) | collective-permute-done | bytes 524320 | tf_op jit(solution)/shard_map/ppermute | solution.py:17
  98.5 2.1 copy.155
  100.6 6.8 %fusion.2 = (bf16[4,2,256,256]{2,3,1,0:T(8,128)(2,1)S(1)}, bf16[4,2,256,256]{2,3,1,0:T(8,128)(2,1)}, bf16[4,2,256,256]{2,3,1,0:T(8,128)(2,1)}) fusion(f32[4,256,256,2]{2,1,3,0:T(8,128)} %get-tuple-element.31, f32[4,2,256,256]{2,3,1,0:T(8,128)} %copy-done.1, f32[4,2,256]{2,1,0:T(2,128)S(1)} %add_divide_fusion, f32[4,2,256]{2,1,0:T(2,128)S(1)} %get-tuple-element.9, ...), kind=kLoop, calls=%fused_computation.4 | loop fusion | flops 6291456 | bytes 15745024 | tf_op jit(solution)/shard_map/convert_element_type | solution.py:98
  111.3 2.2 pad_maximum_fusion
  113.5 2.3 collective-permute-start.2
  115.8 2.2 pad_maximum_fusion.1
  118.1 5.2 %collective-permute-start.3 = (f32[2,256,512]{2,1,0:T(8,128)}, f32[2,256,512]{2,1,0:T(8,128)}, u32[]{:S(2)}, u32[]{:S(2)}) collective-permute-start(f32[2,256,512]{2,1,0:T(8,128)} %pad_maximum_fusion.1), channel_id=1, source_target_pairs={{8,0},{12,4},{16,8},{20,12},{24,16},{28,20},{32,24},{36,28},{40,32... | collective-permute-start | bytes 3145736 | tf_op jit(solution)/shard_map/ppermute | solution.py:17
  127.4 3.6 %all-to-all-start.4 = ((bf16[4,64,1024]{2,1,0:T(8,128)(2,1)}), bf16[4,64,1024]{2,1,0:T(8,128)(2,1)S(1)}, u32[]{:S(2)}, u32[]{:S(2)}) async-start(bf16[4,64,1024]{2,1,0:T(8,128)(2,1)} %convert_element_type.39), calls=%async_computation.4 | async-start | bytes 1048576 | tf_op jit(solution)/shard_map/all_to_all | solution.py:124
  131.7 42.0 %collective-permute-done.2 = f32[2,256,512]{2,1,0:T(8,128)} collective-permute-done((f32[2,256,512]{2,1,0:T(8,128)}, f32[2,256,512]{2,1,0:T(8,128)}, u32[]{:S(2)}, u32[]{:S(2)}) %collective-permute-start.2) | collective-permute-done | bytes 1048608 | tf_op jit(solution)/shard_map/ppermute | solution.py:17
  173.7 57.3 %collective-permute-done.3 = f32[2,256,512]{2,1,0:T(8,128)} collective-permute-done((f32[2,256,512]{2,1,0:T(8,128)}, f32[2,256,512]{2,1,0:T(8,128)}, u32[]{:S(2)}, u32[]{:S(2)}) %collective-permute-start.3) | collective-permute-done | bytes 1048608 | tf_op jit(solution)/shard_map/ppermute | solution.py:17
  233.5 10.2 %all_to_all.112 = bf16[4,64,512]{2,1,0:T(8,128)(2,1)S(1)} all-to-all(bf16[4,64,512]{2,1,0:T(8,128)(2,1)S(1)} %bitcast.204), channel_id=1, replica_groups=mesh['ctx'=128,'head'=4] {'head'}, dimensions={0} | all-to-all | bytes 524288 | tf_op jit(solution)/shard_map/all_to_all | solution.py:125
  243.8 3.4 %all-to-all-start.6 = ((bf16[4,64,512]{2,1,0:T(8,128)(2,1)}), bf16[4,64,512]{2,1,0:T(8,128)(2,1)S(1)}, u32[]{:S(2)}, u32[]{:S(2)}) async-start(bf16[4,64,512]{2,1,0:T(8,128)(2,1)} %bitcast.57), calls=%async_computation.6 | async-start | bytes 524288 | tf_op jit(solution)/shard_map/all_to_all | solution.py:126
  248.8 4.4 %all-to-all-done.6 = bf16[4,64,512]{2,1,0:T(8,128)(2,1)S(1)} async-done(((bf16[4,64,512]{2,1,0:T(8,128)(2,1)}), bf16[4,64,512]{2,1,0:T(8,128)(2,1)S(1)}, u32[]{:S(2)}, u32[]{:S(2)}) %all-to-all-start.6) | async-done | bytes 262176 | tf_op jit(solution)/shard_map/all_to_all | solution.py:126
  (85 shorter events, 48.9 us)
Async XLA Ops:
  0.6 14.8 %copy-start.13 = (bf16[64,4096]{1,0:T(8,128)(2,1)S(1)}, bf16[64,4096]{1,0:T(8,128)(2,1)}, u32[]{:S(2)}) copy-start(bf16[64,4096]{1,0:T(8,128)(2,1)} %param.5) | copy-start | bytes 1572868
  0.6 24.3 %copy-start.14 = (bf16[64,4096]{1,0:T(8,128)(2,1)S(1)}, bf16[64,4096]{1,0:T(8,128)(2,1)}, u32[]{:S(2)}) copy-start(bf16[64,4096]{1,0:T(8,128)(2,1)} %param.8) | copy-start | bytes 1572868
  2.4 9.6 %all-to-all-start = ((bf16[64,4,512]{2,0,1:T(8,128)(2,1)}), bf16[64,4,512]{2,0,1:T(8,128)(2,1)S(1)}, u32[]{:S(2)}, u32[]{:S(2)}) async-start(bf16[64,4,512]{2,0,1:T(8,128)(2,1)} %bitcast.174), calls=%async_computation | async-start | bytes 524288 | tf_op jit(solution)/shard_map/all_to_all | solution.py:29
  12.1 9.4 %all-to-all-start.2 = ((bf16[64,4,512]{2,0,1:T(8,128)(2,1)}), bf16[64,4,512]{2,0,1:T(8,128)(2,1)S(1)}, u32[]{:S(2)}, u32[]{:S(2)}) async-start(bf16[64,4,512]{2,0,1:T(8,128)(2,1)} %bitcast.173), calls=%async_computation.2 | async-start | bytes 524288 | tf_op jit(solution)/shard_map/all_to_all | solution.py:30
  15.5 21.7 %copy-start.16 = (s32[256]{0:T(256)S(1)}, s32[256]{0:T(256)}, u32[]{:S(2)}) copy-start(s32[256]{0:T(256)} %param.9) | copy-start | bytes 3076
  21.4 12.3 %all-to-all-start.1 = ((bf16[64,4,1024]{2,0,1:T(8,128)(2,1)}), bf16[64,4,1024]{2,0,1:T(8,128)(2,1)S(1)}, u32[]{:S(2)}, u32[]{:S(2)}) async-start(bf16[64,4,1024]{2,0,1:T(8,128)(2,1)} %bitcast.172), calls=%async_computation.1 | async-start | bytes 1048576 | tf_op jit(solution)/shard_map/all_to_all | solution.py:28
  33.7 15.8 %all-to-all-start.3 = ((bf16[64,4,1024]{2,0,1:T(8,128)(2,1)}), bf16[64,4,1024]{2,0,1:T(8,128)(2,1)S(1)}, u32[]{:S(2)}, u32[]{:S(2)}) async-start(bf16[64,4,1024]{2,0,1:T(8,128)(2,1)} %bitcast.171), calls=%async_computation.3 | async-start | bytes 1048576 | tf_op jit(solution)/shard_map/all_to_all | solution.py:31
  38.9 29.6 %collective-permute-start.1 = (bf16[2,256,512]{2,1,0:T(8,128)(2,1)}, bf16[2,256,512]{2,1,0:T(8,128)(2,1)}, u32[]{:S(2)}, u32[]{:S(2)}) collective-permute-start(bf16[2,256,512]{2,1,0:T(8,128)(2,1)} %pad_maximum_fusion.2), channel_id=1, source_target_pairs={{0,8},{4,12},{8,16},{12,20},{16,24},{20,28},{24,32},{28,36},{32,40... | collective-permute-start | bytes 1572872 | tf_op jit(solution)/shard_map/ppermute | solution.py:17
  44.3 35.0 %collective-permute-start = (bf16[2,256,512]{2,1,0:T(8,128)(2,1)}, bf16[2,256,512]{2,1,0:T(8,128)(2,1)}, u32[]{:S(2)}, u32[]{:S(2)}) collective-permute-start(bf16[2,256,512]{2,1,0:T(8,128)(2,1)} %pad_maximum_fusion.2), channel_id=1, source_target_pairs={{0,4},{4,8},{8,12},{12,16},{16,20},{20,24},{24,28},{28,32},{32,36}... | collective-permute-start | bytes 1572872 | tf_op jit(solution)/shard_map/ppermute | solution.py:17
  50.4 1.4 copy-start.12
  84.7 1.5 copy-start.6
  86.2 6.4 %copy-start = (f32[4,2,256,256]{2,3,1,0:T(8,128)}, f32[4,2,256,256]{2,3,1,0:T(8,128)S(1)}, u32[]{:S(2)}) copy-start(f32[4,2,256,256]{2,3,1,0:T(8,128)S(1)} %get-tuple-element.30) | copy-start | bytes 6291460
  86.7 7.1 %copy-start.1 = (f32[4,2,256,256]{2,3,1,0:T(8,128)}, f32[4,2,256,256]{2,3,1,0:T(8,128)S(1)}, u32[]{:S(2)}) copy-start(f32[4,2,256,256]{2,3,1,0:T(8,128)S(1)} %get-tuple-element.26) | copy-start | bytes 6291460
  87.3 1.9 copy-start.11
  89.3 2.0 copy-start.15
  107.4 2.5 copy-start.3
  111.3 11.9 %copy-start.2 = (bf16[4,2,256,256]{2,3,1,0:T(8,128)(2,1)S(1)}, bf16[4,2,256,256]{2,3,1,0:T(8,128)(2,1)}, u32[]{:S(2)}) copy-start(bf16[4,2,256,256]{2,3,1,0:T(8,128)(2,1)} %get-tuple-element.21) | copy-start | bytes 3145732
  113.5 10.3 %copy-start.8 = (bf16[1,256,512]{1,2,0:T(8,128)(2,1)S(1)}, bf16[1,256,512]{1,2,0:T(8,128)(2,1)}, u32[]{:S(2)}) copy-start(bf16[1,256,512]{1,2,0:T(8,128)(2,1)} %copy.127) | copy-start | bytes 786436
  113.5 60.1 %collective-permute-start.2 = (f32[2,256,512]{2,1,0:T(8,128)}, f32[2,256,512]{2,1,0:T(8,128)}, u32[]{:S(2)}, u32[]{:S(2)}) collective-permute-start(f32[2,256,512]{2,1,0:T(8,128)} %pad_maximum_fusion), channel_id=1, source_target_pairs={{4,0},{8,4},{12,8},{16,12},{20,16},{24,20},{28,24},{32,28},{36,32}... | collective-permute-start | bytes 3145736 | tf_op jit(solution)/shard_map/ppermute | solution.py:17
  118.1 112.9 %collective-permute-start.3 = (f32[2,256,512]{2,1,0:T(8,128)}, f32[2,256,512]{2,1,0:T(8,128)}, u32[]{:S(2)}, u32[]{:S(2)}) collective-permute-start(f32[2,256,512]{2,1,0:T(8,128)} %pad_maximum_fusion.1), channel_id=1, source_target_pairs={{8,0},{12,4},{16,8},{20,12},{24,16},{28,20},{32,24},{36,28},{40,32... | collective-permute-start | bytes 3145736 | tf_op jit(solution)/shard_map/ppermute | solution.py:17
  123.9 1.3 copy-start.7
  127.4 103.6 %copy-start.9 = (f32[1,256,512]{2,1,0:T(8,128)S(1)}, f32[1,256,512]{2,1,0:T(8,128)}, u32[]{:S(2)}) copy-start(f32[1,256,512]{2,1,0:T(8,128)} %copy.155) | copy-start | bytes 1572868
  127.4 106.2 %all-to-all-start.4 = ((bf16[4,64,1024]{2,1,0:T(8,128)(2,1)}), bf16[4,64,1024]{2,1,0:T(8,128)(2,1)S(1)}, u32[]{:S(2)}, u32[]{:S(2)}) async-start(bf16[4,64,1024]{2,1,0:T(8,128)(2,1)} %convert_element_type.39), calls=%async_computation.4 | async-start | bytes 1048576 | tf_op jit(solution)/shard_map/all_to_all | solution.py:124
  243.8 9.4 %all-to-all-start.6 = ((bf16[4,64,512]{2,1,0:T(8,128)(2,1)}), bf16[4,64,512]{2,1,0:T(8,128)(2,1)S(1)}, u32[]{:S(2)}, u32[]{:S(2)}) async-start(bf16[4,64,512]{2,1,0:T(8,128)(2,1)} %bitcast.57), calls=%async_computation.6 | async-start | bytes 524288 | tf_op jit(solution)/shard_map/all_to_all | solution.py:126
  (3 other events, 3.4 us)
where the time goes:
time: 255 us; the launch traced here: 254 us
  waiting for transfers between devices  141 us (55%)
  starting transfers between devices  37.3 us (15%)
  local copies, waits for them, and re-layouts  33.3 us (13%)
  matrix products  16.5 us (6%)
  other arithmetic  14.8 us (6%)
  blocking collectives  10.2 us (4%)
    ppermute x4, waiting for transfers between devices, passed_along(): return lax.ppermute(block, axis, route)  119 us
    ppermute x4, starting transfers between devices, passed_along(): return lax.ppermute(block, axis, route)  16.3 us
    all_to_all x1, blocking collectives, local(): lax.all_to_all(grad_key_loc, 'head', split_axis=0, concat_axis=1, tiled=T...  10.2 us
    all_to_all x1, waiting for transfers between devices, local(): lax.all_to_all(queries, 'head', split_axis=1, concat_axis=0, tiled=True)  7.94 us
    another operation x6, local copies, waits for them, and re-layouts, local(): jnp.stack([key_part, value_part])  7.59 us
    slice x4, local copies, waits for them, and re-layouts, unpack(): kv_block[1].reshape(tok_rows, kv_groups, HEAD_SIZE)  7.31 us
    convert_element_type x1, other arithmetic, local(): dscore = (prob * (dprob - delta[..., None])).astype(jnp.bfloat16)  6.79 us
    all_to_all x1, waiting for transfers between devices, local(): lax.all_to_all(value_state_rows, 'head', split_axis=1, concat_axis=0, til...  5.12 us
  transfers between devices with their start and end apart: 10, of which 8 were waited for; matrix products, arithmetic and copies ran while one was open for 11% of the time, Pallas kernels for 0%

commit v1 on v0

--- a/solution.py
+++ b/solution.py
@@ -9,6 +9,12 @@
 WINDOW = 512
 SPAN = 2
 score_scale = 168.0 ** (-0.5)
+
+
+def trade_parts(shard, mesh_axis, split, join):
+    pieces = jnp.split(shard, lax.axis_size(mesh_axis), axis=split)
+    got = lax.all_to_all(jnp.stack(pieces), mesh_axis, 0, 0)
+    return jnp.concatenate(got, axis=join)
 
 
 def passed_along(block, axis, distance):
@@ -25,7 +31,7 @@
 
 def local(queries, normed_key_state, value_state_rows, output_gradient, doc_start):
     query_loc, key_loc, value_loc, grad_loc = (
-        lax.all_to_all(queries, "head", split_axis=1, concat_axis=0, tiled=True),
+        trade_parts(queries, "head", 1, 0),
         lax.all_to_all(normed_key_state, "head", split_axis=1, concat_axis=0, tiled=True),
         lax.all_to_all(value_state_rows, "head", split_axis=1, concat_axis=0, tiled=True),
         lax.all_to_all(output_gradient, "head", split_axis=1, concat_axis=0, tiled=True),

time: 255 us -> 255 us (level)
    all_to_all x1, waiting for transfers between devices: 7.94 us -> 0.01 us  [trade_parts(): got = lax.all_to_all(jnp.stack(pieces), mesh_axis, 0, 0)]
    all_to_all x1, waiting for transfers between devices: 0.01 us -> 7.85 us  [local(): lax.all_to_all(output_gradient, 'head', split_axis=1, concat_axis=0, tile...]
where the time goes in v1:
time: 255 us; the launch traced here: 254 us
  waiting for transfers between devices  141 us (55%)
  starting transfers between devices  37.4 us (15%)
  local copies, waits for them, and re-layouts  32.5 us (13%)
  matrix products  16.5 us (6%)
  other arithmetic  15.7 us (6%)
  blocking collectives  10.3 us (4%)
    ppermute x4, waiting for transfers between devices, passed_along(): return lax.ppermute(block, axis, route)  119 us
    ppermute x4, starting transfers between devices, passed_along(): return lax.ppermute(block, axis, route)  16.3 us
    all_to_all x1, blocking collectives, local(): lax.all_to_all(grad_key_loc, 'head', split_axis=0, concat_axis=1, tiled=T...  10.3 us
    all_to_all x1, waiting for transfers between devices, local(): lax.all_to_all(output_gradient, 'head', split_axis=1, concat_axis=0, tile...  7.85 us
    another operation x6, local copies, waits for them, and re-layouts, local(): jnp.stack([key_part, value_part])  7.57 us
    slice x4, local copies, waits for them, and re-layouts, unpack(): kv_block[1].reshape(tok_rows, kv_groups, HEAD_SIZE)  7.29 us
    convert_element_type x1, other arithmetic, local(): dscore = (prob * (dprob - delta[..., None])).astype(jnp.bfloat16)  6.77 us
    all_to_all x1, waiting for transfers between devices, local(): lax.all_to_all(value_state_rows, 'head', split_axis=1, concat_axis=0, til...  5.13 us
  transfers between devices with their start and end apart: 10, of which 8 were waited for; matrix products, arithmetic and copies ran while one was open for 11% of the time, Pallas kernels for 0%

profile of v1, /device:TPU:54, one launch (start us, length us, event | category | flops | bytes accessed | tf_op | source)
XLA Modules:
  0.0 254.0 jit_solution(2645881485803664817)
XLA Ops:
  2.4 3.6 %all-to-all-start.1 = ((bf16[64,4,512]{2,0,1:T(8,128)(2,1)}), bf16[64,4,512]{2,0,1:T(8,128)(2,1)S(1)}, u32[]{:S(2)}, u32[]{:S(2)}) async-start(bf16[64,4,512]{2,0,1:T(8,128)(2,1)} %bitcast.192), calls=%async_computation.1 | async-start | bytes 524288 | tf_op jit(solution)/shard_map/all_to_all | solution.py:35
  7.7 4.3 %all-to-all-done.1 = bf16[64,4,512]{2,0,1:T(8,128)(2,1)S(1)} async-done(((bf16[64,4,512]{2,0,1:T(8,128)(2,1)}), bf16[64,4,512]{2,0,1:T(8,128)(2,1)S(1)}, u32[]{:S(2)}, u32[]{:S(2)}) %all-to-all-start.1) | async-done | bytes 262176 | tf_op jit(solution)/shard_map/all_to_all | solution.py:35
  12.1 3.4 %all-to-all-start.2 = ((bf16[64,4,512]{2,0,1:T(8,128)(2,1)}), bf16[64,4,512]{2,0,1:T(8,128)(2,1)S(1)}, u32[]{:S(2)}, u32[]{:S(2)}) async-start(bf16[64,4,512]{2,0,1:T(8,128)(2,1)} %bitcast.191), calls=%async_computation.2 | async-start | bytes 524288 | tf_op jit(solution)/shard_map/all_to_all | solution.py:36
  16.3 5.1 %all-to-all-done.2 = bf16[64,4,512]{2,0,1:T(8,128)(2,1)S(1)} async-done(((bf16[64,4,512]{2,0,1:T(8,128)(2,1)}), bf16[64,4,512]{2,0,1:T(8,128)(2,1)S(1)}, u32[]{:S(2)}, u32[]{:S(2)}) %all-to-all-start.2) | async-done | bytes 262176 | tf_op jit(solution)/shard_map/all_to_all | solution.py:36
  21.4 3.6 %all-to-all-start.3 = ((bf16[64,4,1024]{2,0,1:T(8,128)(2,1)}), bf16[64,4,1024]{2,0,1:T(8,128)(2,1)S(1)}, u32[]{:S(2)}, u32[]{:S(2)}) async-start(bf16[64,4,1024]{2,0,1:T(8,128)(2,1)} %bitcast.190), calls=%async_computation.3 | async-start | bytes 1048576 | tf_op jit(solution)/shard_map/all_to_all | solution.py:37
  26.0 7.9 %all-to-all-done.3 = bf16[64,4,1024]{2,0,1:T(8,128)(2,1)S(1)} async-done(((bf16[64,4,1024]{2,0,1:T(8,128)(2,1)}), bf16[64,4,1024]{2,0,1:T(8,128)(2,1)S(1)}, u32[]{:S(2)}, u32[]{:S(2)}) %all-to-all-start.3) | async-done | bytes 524320 | tf_op jit(solution)/shard_map/all_to_all | solution.py:37
  33.8 3.5 %all-to-all-start = ((bf16[4,64,1024]{2,1,0:T(8,128)(2,1)}), bf16[4,64,1024]{2,1,0:T(8,128)(2,1)S(1)}, u32[]{:S(2)}, u32[]{:S(2)}) async-start(bf16[4,64,1024]{2,1,0:T(8,128)(2,1)} %pad_maximum_fusion.2), calls=%async_computation | async-start | bytes 1048576 | tf_op jit(solution)/shard_map/all_to_all | solution.py:16
  39.1 5.3 %collective-permute-start.1 = (bf16[2,256,512]{2,1,0:T(8,128)(2,1)}, bf16[2,256,512]{2,1,0:T(8,128)(2,1)}, u32[]{:S(2)}, u32[]{:S(2)}) collective-permute-start(bf16[2,256,512]{2,1,0:T(8,128)(2,1)} %pad_maximum_fusion.3), channel_id=1, source_target_pairs={{0,8},{4,12},{8,16},{12,20},{16,24},{20,28},{24,32},{28,36},{32,40... | collective-permute-start | bytes 1572872 | tf_op jit(solution)/shard_map/ppermute | solution.py:23
  44.4 3.5 %collective-permute-start = (bf16[2,256,512]{2,1,0:T(8,128)(2,1)}, bf16[2,256,512]{2,1,0:T(8,128)(2,1)}, u32[]{:S(2)}, u32[]{:S(2)}) collective-permute-start(bf16[2,256,512]{2,1,0:T(8,128)(2,1)} %pad_maximum_fusion.3), channel_id=1, source_target_pairs={{0,4},{4,8},{8,12},{12,16},{16,20},{20,24},{24,28},{28,32},{32,36}... | collective-permute-start | bytes 1572872 | tf_op jit(solution)/shard_map/ppermute | solution.py:23
  51.9 2.4 fusion.6
  54.3 14.3 %collective-permute-done.1 = bf16[2,256,512]{2,1,0:T(8,128)(2,1)} collective-permute-done((bf16[2,256,512]{2,1,0:T(8,128)(2,1)}, bf16[2,256,512]{2,1,0:T(8,128)(2,1)}, u32[]{:S(2)}, u32[]{:S(2)}) %collective-permute-start.1) | collective-permute-done | bytes 524320 | tf_op jit(solution)/shard_map/ppermute | solution.py:23
  74.1 5.3 %collective-permute-done = bf16[2,256,512]{2,1,0:T(8,128)(2,1)} collective-permute-done((bf16[2,256,512]{2,1,0:T(8,128)(2,1)}, bf16[2,256,512]{2,1,0:T(8,128)(2,1)}, u32[]{:S(2)}, u32[]{:S(2)}) %collective-permute-start) | collective-permute-done | bytes 524320 | tf_op jit(solution)/shard_map/ppermute | solution.py:23
  97.4 2.1 copy.152
  100.7 6.8 %fusion.2 = (bf16[4,2,256,256]{2,3,1,0:T(8,128)(2,1)S(1)}, bf16[4,2,256,256]{2,3,1,0:T(8,128)(2,1)}, bf16[4,2,256,256]{2,3,1,0:T(8,128)(2,1)}) fusion(f32[4,256,256,2]{2,1,3,0:T(8,128)} %get-tuple-element.35, f32[4,2,256,256]{2,3,1,0:T(8,128)} %copy-done.1, f32[4,2,256]{2,1,0:T(2,128)S(1)} %add_divide_fusion, f32[4,2,256]{2,1,0:T(2,128)S(1)} %get-tuple-element.9, ...), kind=kLoop, calls=%fused_computation.4 | loop fusion | flops 6291456 | bytes 15745024 | tf_op jit(solution)/shard_map/convert_element_type | solution.py:104
  111.5 2.2 pad_maximum_fusion
  113.6 2.3 collective-permute-start.2
  115.9 2.2 pad_maximum_fusion.1
  118.2 5.2 %collective-permute-start.3 = (f32[2,256,512]{2,1,0:T(8,128)}, f32[2,256,512]{2,1,0:T(8,128)}, u32[]{:S(2)}, u32[]{:S(2)}) collective-permute-start(f32[2,256,512]{2,1,0:T(8,128)} %pad_maximum_fusion.1), channel_id=1, source_target_pairs={{8,0},{12,4},{16,8},{20,12},{24,16},{28,20},{32,24},{36,28},{40,32... | collective-permute-start | bytes 3145736 | tf_op jit(solution)/shard_map/ppermute | solution.py:23
  127.5 3.6 %all-to-all-start.4 = ((bf16[4,64,1024]{2,1,0:T(8,128)(2,1)}), bf16[4,64,1024]{2,1,0:T(8,128)(2,1)S(1)}, u32[]{:S(2)}, u32[]{:S(2)}) async-start(bf16[4,64,1024]{2,1,0:T(8,128)(2,1)} %convert_element_type.39), calls=%async_computation.4 | async-start | bytes 1048576 | tf_op jit(solution)/shard_map/all_to_all | solution.py:130
  131.8 42.0 %collective-permute-done.2 = f32[2,256,512]{2,1,0:T(8,128)} collective-permute-done((f32[2,256,512]{2,1,0:T(8,128)}, f32[2,256,512]{2,1,0:T(8,128)}, u32[]{:S(2)}, u32[]{:S(2)}) %collective-permute-start.2) | collective-permute-done | bytes 1048608 | tf_op jit(solution)/shard_map/ppermute | solution.py:23
  173.8 57.2 %collective-permute-done.3 = f32[2,256,512]{2,1,0:T(8,128)} collective-permute-done((f32[2,256,512]{2,1,0:T(8,128)}, f32[2,256,512]{2,1,0:T(8,128)}, u32[]{:S(2)}, u32[]{:S(2)}) %collective-permute-start.3) | collective-permute-done | bytes 1048608 | tf_op jit(solution)/shard_map/ppermute | solution.py:23
  233.6 10.3 %all_to_all.101 = bf16[4,64,512]{2,1,0:T(8,128)(2,1)S(1)} all-to-all(bf16[4,64,512]{2,1,0:T(8,128)(2,1)S(1)} %bitcast.221), channel_id=1, replica_groups=mesh['ctx'=128,'head'=4] {'head'}, dimensions={0} | all-to-all | bytes 524288 | tf_op jit(solution)/shard_map/all_to_all | solution.py:131
  243.9 3.4 %all-to-all-start.6 = ((bf16[4,64,512]{2,1,0:T(8,128)(2,1)}), bf16[4,64,512]{2,1,0:T(8,128)(2,1)S(1)}, u32[]{:S(2)}, u32[]{:S(2)}) async-start(bf16[4,64,512]{2,1,0:T(8,128)(2,1)} %bitcast.60), calls=%async_computation.6 | async-start | bytes 524288 | tf_op jit(solution)/shard_map/all_to_all | solution.py:132
  248.8 4.4 %all-to-all-done.6 = bf16[4,64,512]{2,1,0:T(8,128)(2,1)S(1)} async-done(((bf16[4,64,512]{2,1,0:T(8,128)(2,1)}), bf16[4,64,512]{2,1,0:T(8,128)(2,1)S(1)}, u32[]{:S(2)}, u32[]{:S(2)}) %all-to-all-start.6) | async-done | bytes 262176 | tf_op jit(solution)/shard_map/all_to_all | solution.py:132
  (86 shorter events, 49.0 us)
Async XLA Ops:
  0.6 14.8 %copy-start.13 = (bf16[64,4096]{1,0:T(8,128)(2,1)S(1)}, bf16[64,4096]{1,0:T(8,128)(2,1)}, u32[]{:S(2)}) copy-start(bf16[64,4096]{1,0:T(8,128)(2,1)} %param.8) | copy-start | bytes 1572868
  0.6 24.4 %copy-start.14 = (bf16[64,4096]{1,0:T(8,128)(2,1)S(1)}, bf16[64,4096]{1,0:T(8,128)(2,1)}, u32[]{:S(2)}) copy-start(bf16[64,4096]{1,0:T(8,128)(2,1)} %param.5) | copy-start | bytes 1572868
  2.4 9.6 %all-to-all-start.1 = ((bf16[64,4,512]{2,0,1:T(8,128)(2,1)}), bf16[64,4,512]{2,0,1:T(8,128)(2,1)S(1)}, u32[]{:S(2)}, u32[]{:S(2)}) async-start(bf16[64,4,512]{2,0,1:T(8,128)(2,1)} %bitcast.192), calls=%async_computation.1 | async-start | bytes 524288 | tf_op jit(solution)/shard_map/all_to_all | solution.py:35
  12.1 9.4 %all-to-all-start.2 = ((bf16[64,4,512]{2,0,1:T(8,128)(2,1)}), bf16[64,4,512]{2,0,1:T(8,128)(2,1)S(1)}, u32[]{:S(2)}, u32[]{:S(2)}) async-start(bf16[64,4,512]{2,0,1:T(8,128)(2,1)} %bitcast.191), calls=%async_computation.2 | async-start | bytes 524288 | tf_op jit(solution)/shard_map/all_to_all | solution.py:36
  21.4 15.9 %copy-start.16 = (s32[256]{0:T(256)S(1)}, s32[256]{0:T(256)}, u32[]{:S(2)}) copy-start(s32[256]{0:T(256)} %param.9) | copy-start | bytes 3076
  21.4 12.4 %all-to-all-start.3 = ((bf16[64,4,1024]{2,0,1:T(8,128)(2,1)}), bf16[64,4,1024]{2,0,1:T(8,128)(2,1)S(1)}, u32[]{:S(2)}, u32[]{:S(2)}) async-start(bf16[64,4,1024]{2,0,1:T(8,128)(2,1)} %bitcast.190), calls=%async_computation.3 | async-start | bytes 1048576 | tf_op jit(solution)/shard_map/all_to_all | solution.py:37
  33.8 15.8 %all-to-all-start = ((bf16[4,64,1024]{2,1,0:T(8,128)(2,1)}), bf16[4,64,1024]{2,1,0:T(8,128)(2,1)S(1)}, u32[]{:S(2)}, u32[]{:S(2)}) async-start(bf16[4,64,1024]{2,1,0:T(8,128)(2,1)} %pad_maximum_fusion.2), calls=%async_computation | async-start | bytes 1048576 | tf_op jit(solution)/shard_map/all_to_all | solution.py:16
  39.1 29.6 %collective-permute-start.1 = (bf16[2,256,512]{2,1,0:T(8,128)(2,1)}, bf16[2,256,512]{2,1,0:T(8,128)(2,1)}, u32[]{:S(2)}, u32[]{:S(2)}) collective-permute-start(bf16[2,256,512]{2,1,0:T(8,128)(2,1)} %pad_maximum_fusion.3), channel_id=1, source_target_pairs={{0,8},{4,12},{8,16},{12,20},{16,24},{20,28},{24,32},{28,36},{32,40... | collective-permute-start | bytes 1572872 | tf_op jit(solution)/shard_map/ppermute | solution.py:23
  44.4 35.0 %collective-permute-start = (bf16[2,256,512]{2,1,0:T(8,128)(2,1)}, bf16[2,256,512]{2,1,0:T(8,128)(2,1)}, u32[]{:S(2)}, u32[]{:S(2)}) collective-permute-start(bf16[2,256,512]{2,1,0:T(8,128)(2,1)} %pad_maximum_fusion.3), channel_id=1, source_target_pairs={{0,4},{4,8},{8,12},{12,16},{16,20},{20,24},{24,28},{28,32},{32,36}... | collective-permute-start | bytes 1572872 | tf_op jit(solution)/shard_map/ppermute | solution.py:23
  50.6 1.4 copy-start.12
  84.8 1.5 copy-start.6
  86.3 5.1 %copy-start = (f32[4,2,256,256]{2,3,1,0:T(8,128)}, f32[4,2,256,256]{2,3,1,0:T(8,128)S(1)}, u32[]{:S(2)}) copy-start(f32[4,2,256,256]{2,3,1,0:T(8,128)S(1)} %get-tuple-element.34) | copy-start | bytes 6291460
  86.9 7.2 %copy-start.1 = (f32[4,2,256,256]{2,3,1,0:T(8,128)}, f32[4,2,256,256]{2,3,1,0:T(8,128)S(1)}, u32[]{:S(2)}) copy-start(f32[4,2,256,256]{2,3,1,0:T(8,128)S(1)} %get-tuple-element.30) | copy-start | bytes 6291460
  87.5 1.9 copy-start.11
  89.4 2.0 copy-start.15
  107.5 2.5 copy-start.3
  111.5 11.9 %copy-start.2 = (bf16[4,2,256,256]{2,3,1,0:T(8,128)(2,1)S(1)}, bf16[4,2,256,256]{2,3,1,0:T(8,128)(2,1)}, u32[]{:S(2)}) copy-start(bf16[4,2,256,256]{2,3,1,0:T(8,128)(2,1)} %get-tuple-element.25) | copy-start | bytes 3145732
  113.6 10.3 %copy-start.8 = (bf16[1,256,512]{1,2,0:T(8,128)(2,1)S(1)}, bf16[1,256,512]{1,2,0:T(8,128)(2,1)}, u32[]{:S(2)}) copy-start(bf16[1,256,512]{1,2,0:T(8,128)(2,1)} %copy.124) | copy-start | bytes 786436
  113.6 60.1 %collective-permute-start.2 = (f32[2,256,512]{2,1,0:T(8,128)}, f32[2,256,512]{2,1,0:T(8,128)}, u32[]{:S(2)}, u32[]{:S(2)}) collective-permute-start(f32[2,256,512]{2,1,0:T(8,128)} %pad_maximum_fusion), channel_id=1, source_target_pairs={{4,0},{8,4},{12,8},{16,12},{20,16},{24,20},{28,24},{32,28},{36,32}... | collective-permute-start | bytes 3145736 | tf_op jit(solution)/shard_map/ppermute | solution.py:23
  118.2 112.9 %collective-permute-start.3 = (f32[2,256,512]{2,1,0:T(8,128)}, f32[2,256,512]{2,1,0:T(8,128)}, u32[]{:S(2)}, u32[]{:S(2)}) collective-permute-start(f32[2,256,512]{2,1,0:T(8,128)} %pad_maximum_fusion.1), channel_id=1, source_target_pairs={{8,0},{12,4},{16,8},{20,12},{24,16},{28,20},{32,24},{36,28},{40,32... | collective-permute-start | bytes 3145736 | tf_op jit(solution)/shard_map/ppermute | solution.py:23
  124.0 1.3 copy-start.7
  127.5 103.6 %copy-start.9 = (f32[1,256,512]{2,1,0:T(8,128)S(1)}, f32[1,256,512]{2,1,0:T(8,128)}, u32[]{:S(2)}) copy-start(f32[1,256,512]{2,1,0:T(8,128)} %copy.152) | copy-start | bytes 1572868
  127.5 106.1 %all-to-all-start.4 = ((bf16[4,64,1024]{2,1,0:T(8,128)(2,1)}), bf16[4,64,1024]{2,1,0:T(8,128)(2,1)S(1)}, u32[]{:S(2)}, u32[]{:S(2)}) async-start(bf16[4,64,1024]{2,1,0:T(8,128)(2,1)} %convert_element_type.39), calls=%async_computation.4 | async-start | bytes 1048576 | tf_op jit(solution)/shard_map/all_to_all | solution.py:130
  243.9 9.4 %all-to-all-start.6 = ((bf16[4,64,512]{2,1,0:T(8,128)(2,1)}), bf16[4,64,512]{2,1,0:T(8,128)(2,1)S(1)}, u32[]{:S(2)}, u32[]{:S(2)}) async-start(bf16[4,64,512]{2,1,0:T(8,128)(2,1)} %bitcast.60), calls=%async_computation.6 | async-start | bytes 524288 | tf_op jit(solution)/shard_map/all_to_all | solution.py:132
  (3 other events, 3.4 us)
